TPU v7x, 256 devices: a whole 4x4x8 slice. The times are simulated.
256 devices in a mesh: gx: 64 (over x, y, z_hi, core), gy: 4 (over z_lo).
Axes of the slice: x: 4, y: 4, z: 8 (z_hi: 2, z_lo: 4; z = z_hi * 4 + z_lo), core: 2. Of those that a mesh axis runs over, the one named last changes fastest.
Arguments:
- features: bfloat16 [64, 4, 2, 8, 8, 8, 128], P('gx', 'gy'), may hold values from -6 to 6
- cotangent: bfloat16 [64, 4, 2, 4, 4, 4, 256], P('gx', 'gy'), may hold values from -6 to 6
- conv_first: bfloat16 [27, 128, 128], replicated, may hold values from -0.109375 to 0.109375
- down_weight: bfloat16 [8, 128, 256], replicated, may hold values from -0.1875 to 0.1875
- conv_second: bfloat16 [27, 256, 256], replicated, may hold values from -0.078125 to 0.078125
- block_count: int32 [64, 4], P('gx', 'gy'), may hold values from 1 to 2, as said below
- neighbours: int32 [64, 4, 2, 26], P('gx', 'gy'), may hold values from -1 to 1, as said below
Outputs:
- output_field: bfloat16 [64, 4, 2, 4, 4, 4, 256], P('gx', 'gy')
- input_grad: bfloat16 [64, 4, 2, 8, 8, 8, 128], P('gx', 'gy')
- grad_first: float32 [27, 128, 128], P(None, 'gx')
- grad_down: float32 [8, 128, 256], P(None, 'gx')
- grad_second: float32 [27, 256, 256], P(None, 'gx')
Inputs may be any that keep to these rules, and one draw needn't show every extreme that they name: `block_count`: each column holds 1 to 2 active blocks at distinct levels of its 8, in slots 0 up to its count in rising level; some column holds exactly 2. neighbours[i, j, s, k] is the slot, in column (i + ox, j + oy), of the active block oz levels from slot s's block, for the k-th nonzero offset (ox, oy, oz) with ox slowest and oz fastest, or -1 where there is none; it is below that column's count; rows of slots at or past block_count[i, j] are all -1; the relation is symmetric.
All inputs are finite; a program needn't handle non-finite values.
Results may differ from a plain program's by a relative error of at most 0.01.
Values may be sent and summed in bfloat16 or wider, within the bound.
No kernel may reach another device: no remote copies, remote signals or barrier semaphores. Data moves between devices by JAX's collectives and lax.ppermute only.
A program may use at most 128 MiB of HBM per device.

v0:
```python
import math
import jax
import jax.numpy as jnp
from jax import lax
from jax.sharding import PartitionSpec as P

NEIGHBOUR_STEPS = (-1, 0, 1)


def as_sent(shard):
    return jax.tree.map(lambda a: a.astype(jnp.bfloat16) if a.dtype == jnp.float32 else a, shard)


def shifted(block, axis, distance):
    devices = range(lax.axis_size(axis))
    route = [(i - distance, i) for i in devices if i - distance in devices]
    return lax.ppermute(block, axis, route)


def column_of(offset_x, offset_y, offset_z):
    raster = 9 * (offset_x + 1) + 3 * (offset_y + 1) + (offset_z + 1)
    return raster - 1 if raster > 13 else raster


def outer_layer(values, axis, border):
    length = values.shape[axis]
    first_index = 0 if border == 0 else length - 1
    return lax.slice_in_dim(values, first_index, first_index + 1, axis=axis)


def share_faces(fields):
    nearby = [dict() for member in fields]
    onward = [dict() for member in fields]
    for stride in (1, -1):
        border = 1 if stride == 1 else 0
        payload = []
        for volume in fields:
            planar = outer_layer(volume, 1, border)
            payload += [planar, outer_layer(planar, 2, 0), outer_layer(planar, 2, 1)]
        arrived = shifted(as_sent(tuple(payload)), "gx", stride)
        member = 0
        nearby[member][-stride, 0] = arrived[3 * member]
        onward[member][-stride, 0] = arrived[3 * member + 1]
        onward[member][-stride, 1] = arrived[3 * member + 2]
    for stride in (1, -1):
        border = 1 if stride == 1 else 0
        payload = []
        member = 0
        payload += [
            outer_layer(fields[member], 2, border),
            onward[member][-1, border],
            onward[member][1, border],
        ]
        arrived = shifted(as_sent(tuple(payload)), "gy", stride)
        member = 0
        nearby[member][0, -stride] = arrived[3 * member]
        nearby[member][-1, -stride] = arrived[3 * member + 1]
        nearby[member][1, -stride] = arrived[3 * member + 2]
    return nearby


def surround(center, nearby, slot_table):
    depth = center.shape[3]
    slabs_x = []
    for offset_x in NEIGHBOUR_STEPS:
        slabs_y = []
        for offset_y in NEIGHBOUR_STEPS:
            source = center if offset_x == 0 and offset_y == 0 else nearby[offset_x, offset_y]
            pieces = []
            for offset_z in NEIGHBOUR_STEPS:
                if offset_x == 0 and offset_y == 0 and (offset_z == 0):
                    pieces.append(center)
                else:
                    slot_ids = slot_table[:, column_of(offset_x, offset_y, offset_z)]
                    picked = jnp.take(source, jnp.maximum(slot_ids, 0), axis=0)
                    picked = jnp.where(
                        (slot_ids >= 0)[:, None, None, None, None],
                        picked,
                        jnp.zeros((), picked.dtype),
                    )
                    if offset_z == -1:
                        picked = picked[:, :, :, depth - 1 :]
                    elif offset_z == 1:
                        picked = picked[:, :, :, :1]
                    pieces.append(picked)
            slabs_y.append(jnp.concatenate(pieces, axis=3))
        slabs_x.append(jnp.concatenate(slabs_y, axis=2))
    return jnp.concatenate(slabs_x, axis=1)


def unfold(padded, extent):
    windows = []
    for along_x in range(3):
        for along_y in range(3):
            for along_z in range(3):
                windows.append(
                    padded[
                        :,
                        along_x : along_x + extent,
                        along_y : along_y + extent,
                        along_z : along_z + extent,
                        :,
                    ]
                )
    stacked = jnp.concatenate(windows, axis=-1)
    return stacked.reshape(-1, stacked.shape[-1])


def into_cells(blocks, half_edge):
    slot_count, channels = (blocks.shape[0], blocks.shape[-1])
    lattice = blocks.reshape(slot_count, half_edge, 2, half_edge, 2, half_edge, 2, channels)
    lattice = lattice.transpose(0, 1, 3, 5, 2, 4, 6, 7)
    return lattice.reshape(slot_count * half_edge**3, 8 * channels)


def from_cells(cell_rows, slot_count, half_edge, channels):
    lattice = cell_rows.reshape(slot_count, half_edge, half_edge, half_edge, 2, 2, 2, channels)
    lattice = lattice.transpose(0, 1, 4, 2, 5, 3, 6, 7)
    return lattice.reshape(slot_count, 2 * half_edge, 2 * half_edge, 2 * half_edge, channels)


def silu_slope(values):
    logistic = jax.nn.sigmoid(values)
    return logistic * (1.0 + values * (1.0 - logistic))


def contract_rows(left, right):
    return lax.dot_general(
        left, right, (((0,), (0,)), ((), ())), preferred_element_type=jnp.float32
    )


def body(features, cotangent, conv_first, down_weight, conv_second, block_count, neighbours):
    inputs = features[0, 0]
    slot_count, extent, channels = (inputs.shape[0], inputs.shape[1], inputs.shape[-1])
    half_edge = extent // 2
    wide_channels = conv_second.shape[-1]
    slot_table = neighbours[0, 0]
    live_mask = (jnp.arange(slot_count) < block_count[0, 0])[:, None, None, None, None]
    inputs = jnp.where(live_mask, inputs, jnp.zeros((), inputs.dtype))
    seed_blocks = jnp.where(live_mask, cotangent[0, 0], jnp.zeros((), inputs.dtype))
    near_input = share_faces((inputs,))[0]
    first_matrix = conv_first.reshape(-1, channels)
    first_cols = unfold(surround(inputs, near_input, slot_table), extent)
    pre_first = jnp.dot(first_cols, first_matrix, preferred_element_type=jnp.float32)
    hidden_first = jax.nn.silu(pre_first).astype(jnp.bfloat16)
    first_cells = into_cells(
        hidden_first.reshape(slot_count, extent, extent, extent, channels), half_edge
    )
    down_matrix = down_weight.reshape(-1, wide_channels)
    pre_down = jnp.dot(first_cells, down_matrix, preferred_element_type=jnp.float32)
    hidden_down = (
        jax.nn.silu(pre_down)
        .astype(jnp.bfloat16)
        .reshape(slot_count, half_edge, half_edge, half_edge, wide_channels)
    )
    near_hidden = share_faces((hidden_down,))[0]
    second_cols = unfold(surround(hidden_down, near_hidden, slot_table), half_edge)
    second_matrix = conv_second.reshape(-1, wide_channels)
    output_field = jnp.dot(second_cols, second_matrix, preferred_element_type=jnp.float32).astype(
        jnp.bfloat16
    )
    near_seed = share_faces((seed_blocks,))[0]
    seed_cols = unfold(surround(seed_blocks, near_seed, slot_table), half_edge)
    second_flip = jnp.transpose(conv_second[::-1], (0, 2, 1)).reshape(-1, wide_channels)
    back_down = jnp.dot(seed_cols, second_flip, preferred_element_type=jnp.float32)
    delta_down = (back_down * silu_slope(pre_down)).astype(jnp.bfloat16)
    grad_second = contract_rows(second_cols, seed_blocks.reshape(-1, wide_channels))
    grad_down = contract_rows(first_cells, delta_down)
    back_cells = lax.dot_general(
        delta_down, down_matrix, (((1,), (1,)), ((), ())), preferred_element_type=jnp.float32
    )
    back_first = from_cells(back_cells, slot_count, half_edge, channels).reshape(-1, channels)
    delta_first = (back_first * silu_slope(pre_first)).astype(jnp.bfloat16)
    delta_blocks = delta_first.reshape(slot_count, extent, extent, extent, channels)
    near_delta = share_faces((delta_blocks,))[0]
    delta_cols = unfold(surround(delta_blocks, near_delta, slot_table), extent)
    first_flip = jnp.transpose(conv_first[::-1], (0, 2, 1)).reshape(-1, channels)
    input_grad = jnp.dot(delta_cols, first_flip, preferred_element_type=jnp.float32).astype(
        jnp.bfloat16
    )
    grad_first = contract_rows(first_cols, delta_first)
    first_term = grad_first.reshape(27, channels, channels)
    down_term = grad_down.reshape(8, channels, wide_channels)
    second_term = grad_second.reshape(27, wide_channels, wide_channels)
    columns = (
        lax.psum_scatter(first_term, "gx", scatter_dimension=1, tiled=True),
        lax.psum_scatter(down_term, "gx", scatter_dimension=1, tiled=True),
        lax.psum_scatter(second_term, "gx", scatter_dimension=1, tiled=True),
    )
    summed = (
        lax.psum(columns[0].astype(jnp.bfloat16), "gy").astype(jnp.float32),
        lax.psum(columns[1].astype(jnp.bfloat16), "gy").astype(jnp.float32),
        lax.psum(columns[2].astype(jnp.bfloat16), "gy").astype(jnp.float32),
    )
    devices = lax.axis_size("gx") * lax.axis_size("gy")
    scale_first = 1.0 / math.sqrt(float(devices * slot_count * extent**3))
    scale_half = 1.0 / math.sqrt(float(devices * slot_count * half_edge**3))
    return (
        output_field.reshape(1, 1, slot_count, half_edge, half_edge, half_edge, wide_channels),
        input_grad.reshape(1, 1, slot_count, extent, extent, extent, channels),
        summed[0] * scale_first,
        summed[1] * scale_half,
        summed[2] * scale_half,
    )


def solution(mesh):
    placed = (
        P("gx", "gy", None, None, None, None, None),
        P("gx", "gy", None, None, None, None, None),
        P(),
        P(),
        P(),
        P("gx", "gy"),
        P("gx", "gy", None, None),
    )
    return jax.shard_map(
        body,
        mesh=mesh,
        in_specs=placed,
        out_specs=(
            P("gx", "gy", None, None, None, None, None),
            P("gx", "gy", None, None, None, None, None),
            P(None, "gx", None),
            P(None, "gx", None),
            P(None, "gx", None),
        ),
        check_vma=False,
    )
```

profile of v0, /device:TPU:2, one launch (start us, length us, event | category | flops | bytes accessed | tf_op | source)
XLA Modules:
  0.0 1120.0 jit_solution(13349509447897729206)
XLA Ops:
  10.9 9.2 collective-permute-start
  20.1 3.7 collective-permute-start.7
  27.4 7.5 collective-permute-start.31
  63.4 4.3 collective-permute-start.1
  67.7 2.9 collective-permute-start.8
  73.2 5.7 copy.23
  79.0 4.2 rev.6
  89.1 4.5 collective-permute-start.29
  100.8 3.6 collective-permute-start.32
  114.8 9.1 collective-permute-start.33
  126.5 5.5 collective-permute-start.25
  134.7 4.6 collective-permute-start.5
  141.2 10.6 collective-permute-start.9
  189.4 3.0 multiply_convert_fusion.1
  194.7 10.3 copy.26
  205.0 3.9 collective-permute-start.17
  208.9 10.3 collective-permute-start.19
  226.4 3.9 collective-permute-start.20
  235.4 3.9 collective-permute-start.13
  240.9 8.6 collective-permute-start.21
  315.6 2.9 reshape.552
  326.5 5.0 fusion.3
  382.1 3.8 copy.29
  386.0 5.4 fusion.61
  392.7 10.6 collective-permute-start.43
  409.6 7.5 collective-permute-start.39
  417.2 3.2 convolution_convert_fusion.1
  420.4 547.1 %all-reduce.8 = (bf16[27,128,128]{2,1,0:T(8,128)(2,1)}, bf16[27,256,256]{2,1,0:T(8,128)(2,1)}) all-reduce(f32[27,128,128]{2,1,0:T(8,128)S(1)} %fusion.3, f32[27,256,256]{2,1,0:T(8,128)} %fusion.61), channel_id=2, replica_groups=mesh['gx'=64,'gy'=4] {'gx'}, use_global_device_ids=true, to_apply=%region_0.9.clone | all-reduce | flops 2211840 | bytes 13271040
  973.1 15.6 %collective-permute-start.37 = (bf16[2,1,1,8,128]{4,3,2,1,0:T(8,128)(2,1)S(1)}, bf16[2,1,1,8,128]{4,3,2,1,0:T(8,128)(2,1)S(1)}, u32[]{:S(2)}, u32[]{:S(2)}) collective-permute-start(bf16[2,1,1,8,128]{4,3,2,1,0:T(8,128)(2,1)S(1)} %collective-permute-done.36), channel_id=1, source_target_pairs={{0,1},{1,2},{2,3},{4,5},{5,6},{6,7},{8,9},{9,10},{10,11},{12,13},{... | collective-permute-start | bytes 12296 | tf_op jit(solution)/shard_map/ppermute | solution.py:17
  992.2 4.5 collective-permute-start.41
  1051.4 5.8 convolution_convert_fusion
  1057.1 51.8 %all-reduce.7.cloned.1.call-done = (bf16[27,2,128]{2,1,0:T(2,128)(2,1)}, bf16[8,2,256]{2,0,1:T(8,128)(2,1)}, bf16[27,4,256]{2,1,0:T(4,128)(2,1)}) async-done(((bf16[27,2,128]{2,1,0:T(2,128)(2,1)}, bf16[8,2,256]{2,0,1:T(8,128)(2,1)}, bf16[27,4,256]{2,1,0:T(4,128)(2,1)}), (bf16[27,2,128]{2,1,0:T(2,128)(2,1)}, bf16[8,2,256]{2,0,1:T(8,128)(2,1)}, bf16[27,4,256]{2,1,0:T(4,128)(2,1)})) %all-reduce.7.cloned.1.call-update) | async-done | bytes 77328 | tf_op jit(solution)/shard_map/psum | solution.py:192
  (751 shorter events, 318.4 us)
Async XLA Ops:
  7.2 1042.8 %reduce-scatter.4.cloned.1.call-start = ((), (), s32[]{:S(2)}) async-start(), calls=%async_computation.1 | async-start | bytes 1064960 | tf_op jit(solution)/shard_map/reduce_scatter | solution.py:188
  9.0 50.6 %collective-permute-start.3 = (bf16[2,1,1,8,128]{4,3,2,1,0:T(8,128)(2,1)S(1)}, bf16[2,1,1,8,128]{4,3,2,1,0:T(8,128)(2,1)S(1)}, u32[]{:S(2)}, u32[]{:S(2)}) collective-permute-start(bf16[2,1,1,8,128]{4,3,2,1,0:T(8,128)(2,1)S(1)} %get-tuple-element.115), channel_id=1, source_target_pairs={{0,4},{4,8},{8,12},{12,16},{16,20},{20,24},{24,28},{28,32},{32,36}... | collective-permute-start | bytes 12296 | tf_op jit(solution)/shard_map/ppermute | solution.py:17
  10.9 50.0 %collective-permute-start = (bf16[2,1,1,8,128]{4,3,2,1,0:T(8,128)(2,1)S(1)}, bf16[2,1,1,8,128]{4,3,2,1,0:T(8,128)(2,1)S(1)}, u32[]{:S(2)}, u32[]{:S(2)}) collective-permute-start(bf16[2,1,1,8,128]{4,3,2,1,0:T(8,128)(2,1)S(1)} %get-tuple-element.116), channel_id=1, source_target_pairs={{0,4},{4,8},{8,12},{12,16},{16,20},{20,24},{24,28},{28,32},{32,36}... | collective-permute-start | bytes 12296 | tf_op jit(solution)/shard_map/ppermute | solution.py:17
  20.1 43.2 %collective-permute-start.7 = (bf16[2,1,1,8,128]{4,3,2,1,0:T(8,128)(2,1)S(1)}, bf16[2,1,1,8,128]{4,3,2,1,0:T(8,128)(2,1)S(1)}, u32[]{:S(2)}, u32[]{:S(2)}) collective-permute-start(bf16[2,1,1,8,128]{4,3,2,1,0:T(8,128)(2,1)S(1)} %get-tuple-element.113), channel_id=1, source_target_pairs={{4,0},{8,4},{12,8},{16,12},{20,16},{24,20},{28,24},{32,28},{36,32}... | collective-permute-start | bytes 12296 | tf_op jit(solution)/shard_map/ppermute | solution.py:17
  23.8 43.8 %collective-permute-start.10 = (bf16[2,1,1,8,128]{4,3,2,1,0:T(8,128)(2,1)S(1)}, bf16[2,1,1,8,128]{4,3,2,1,0:T(8,128)(2,1)S(1)}, u32[]{:S(2)}, u32[]{:S(2)}) collective-permute-start(bf16[2,1,1,8,128]{4,3,2,1,0:T(8,128)(2,1)S(1)} %get-tuple-element.114), channel_id=1, source_target_pairs={{4,0},{8,4},{12,8},{16,12},{20,16},{24,20},{28,24},{32,28},{36,32}... | collective-permute-start | bytes 12296 | tf_op jit(solution)/shard_map/ppermute | solution.py:17
  27.4 71.0 %collective-permute-start.31 = (bf16[2,1,1,4,256]{4,3,2,1,0:T(4,128)(2,1)S(1)}, bf16[2,1,1,4,256]{4,3,2,1,0:T(4,128)(2,1)S(1)}, u32[]{:S(2)}, u32[]{:S(2)}) collective-permute-start(bf16[2,1,1,4,256]{4,3,2,1,0:T(4,128)(2,1)S(1)} %get-tuple-element.149), channel_id=1, source_target_pairs={{4,0},{8,4},{12,8},{16,12},{20,16},{24,20},{28,24},{32,28},{36,32}... | collective-permute-start | bytes 12296 | tf_op jit(solution)/shard_map/ppermute | solution.py:17
  61.0 39.9 %collective-permute-start.34 = (bf16[2,1,1,4,256]{4,3,2,1,0:T(4,128)(2,1)S(1)}, bf16[2,1,1,4,256]{4,3,2,1,0:T(4,128)(2,1)S(1)}, u32[]{:S(2)}, u32[]{:S(2)}) collective-permute-start(bf16[2,1,1,4,256]{4,3,2,1,0:T(4,128)(2,1)S(1)} %get-tuple-element.150), channel_id=1, source_target_pairs={{4,0},{8,4},{12,8},{16,12},{20,16},{24,20},{28,24},{32,28},{36,32}... | collective-permute-start | bytes 12296 | tf_op jit(solution)/shard_map/ppermute | solution.py:17
  63.4 25.7 %collective-permute-start.1 = (bf16[2,1,1,8,128]{4,3,2,1,0:T(8,128)(2,1)S(1)}, bf16[2,1,1,8,128]{4,3,2,1,0:T(8,128)(2,1)S(1)}, u32[]{:S(2)}, u32[]{:S(2)}) collective-permute-start(bf16[2,1,1,8,128]{4,3,2,1,0:T(8,128)(2,1)S(1)} %collective-permute-done), channel_id=1, source_target_pairs={{0,1},{1,2},{2,3},{4,5},{5,6},{6,7},{8,9},{9,10},{10,11},{12,13},{... | collective-permute-start | bytes 12296 | tf_op jit(solution)/shard_map/ppermute | solution.py:17
  67.7 27.7 %collective-permute-start.8 = (bf16[2,1,1,8,128]{4,3,2,1,0:T(8,128)(2,1)S(1)}, bf16[2,1,1,8,128]{4,3,2,1,0:T(8,128)(2,1)S(1)}, u32[]{:S(2)}, u32[]{:S(2)}) collective-permute-start(bf16[2,1,1,8,128]{4,3,2,1,0:T(8,128)(2,1)S(1)} %collective-permute-done.7), channel_id=1, source_target_pairs={{0,1},{1,2},{2,3},{4,5},{5,6},{6,7},{8,9},{9,10},{10,11},{12,13},{... | collective-permute-start | bytes 12296 | tf_op jit(solution)/shard_map/ppermute | solution.py:17
  70.6 33.9 %collective-permute-start.11 = (bf16[2,1,1,8,128]{4,3,2,1,0:T(8,128)(2,1)S(1)}, bf16[2,1,1,8,128]{4,3,2,1,0:T(8,128)(2,1)S(1)}, u32[]{:S(2)}, u32[]{:S(2)}) collective-permute-start(bf16[2,1,1,8,128]{4,3,2,1,0:T(8,128)(2,1)S(1)} %collective-permute-done.10), channel_id=1, source_target_pairs={{1,0},{2,1},{3,2},{5,4},{6,5},{7,6},{9,8},{10,9},{11,10},{13,12},{... | collective-permute-start | bytes 12296 | tf_op jit(solution)/shard_map/ppermute | solution.py:17
  89.1 50.1 %collective-permute-start.29 = (bf16[2,4,1,4,256]{4,3,2,1,0:T(4,128)(2,1)S(1)}, bf16[2,4,1,4,256]{4,3,2,1,0:T(4,128)(2,1)S(1)}, u32[]{:S(2)}, u32[]{:S(2)}) collective-permute-start(bf16[2,4,1,4,256]{4,3,2,1,0:T(4,128)(2,1)S(1)} %get-tuple-element.155), channel_id=1, source_target_pairs={{0,1},{1,2},{2,3},{4,5},{5,6},{6,7},{8,9},{9,10},{10,11},{12,13},{... | collective-permute-start | bytes 49160 | tf_op jit(solution)/shard_map/ppermute | solution.py:17
  98.4 25.5 %collective-permute-start.24 = (bf16[2,1,1,4,256]{4,3,2,1,0:T(4,128)(2,1)S(1)}, bf16[2,1,1,4,256]{4,3,2,1,0:T(4,128)(2,1)S(1)}, u32[]{:S(2)}, u32[]{:S(2)}) collective-permute-start(bf16[2,1,1,4,256]{4,3,2,1,0:T(4,128)(2,1)S(1)} %get-tuple-element.152), channel_id=1, source_target_pairs={{0,4},{4,8},{8,12},{12,16},{16,20},{20,24},{24,28},{28,32},{32,36}... | collective-permute-start | bytes 12296 | tf_op jit(solution)/shard_map/ppermute | solution.py:17
  100.8 24.4 %collective-permute-start.32 = (bf16[2,1,1,4,256]{4,3,2,1,0:T(4,128)(2,1)S(1)}, bf16[2,1,1,4,256]{4,3,2,1,0:T(4,128)(2,1)S(1)}, u32[]{:S(2)}, u32[]{:S(2)}) collective-permute-start(bf16[2,1,1,4,256]{4,3,2,1,0:T(4,128)(2,1)S(1)} %collective-permute-done.31), channel_id=1, source_target_pairs={{0,1},{1,2},{2,3},{4,5},{5,6},{6,7},{8,9},{9,10},{10,11},{12,13},{... | collective-permute-start | bytes 12296 | tf_op jit(solution)/shard_map/ppermute | solution.py:17
  114.8 26.4 %collective-permute-start.33 = (bf16[2,1,4,4,256]{4,3,2,1,0:T(4,128)(2,1)S(1)}, bf16[2,1,4,4,256]{4,3,2,1,0:T(4,128)(2,1)S(1)}, u32[]{:S(2)}, u32[]{:S(2)}) collective-permute-start(bf16[2,1,4,4,256]{4,3,2,1,0:T(4,128)(2,1)S(1)} %get-tuple-element.153), channel_id=1, source_target_pairs={{4,0},{8,4},{12,8},{16,12},{20,16},{24,20},{28,24},{32,28},{36,32}... | collective-permute-start | bytes 49160 | tf_op jit(solution)/shard_map/ppermute | solution.py:17
  123.9 27.9 %collective-permute-start.30 = (bf16[2,4,1,4,256]{4,3,2,1,0:T(4,128)(2,1)S(1)}, bf16[2,4,1,4,256]{4,3,2,1,0:T(4,128)(2,1)S(1)}, u32[]{:S(2)}, u32[]{:S(2)}) collective-permute-start(bf16[2,4,1,4,256]{4,3,2,1,0:T(4,128)(2,1)S(1)} %get-tuple-element.156), channel_id=1, source_target_pairs={{1,0},{2,1},{3,2},{5,4},{6,5},{7,6},{9,8},{10,9},{11,10},{13,12},{... | collective-permute-start | bytes 49160 | tf_op jit(solution)/shard_map/ppermute | solution.py:17
  133.4 35.1 %collective-permute-start.6 = (bf16[2,8,1,8,128]{4,3,2,1,0:T(8,128)(2,1)S(1)}, bf16[2,8,1,8,128]{4,3,2,1,0:T(8,128)(2,1)S(1)}, u32[]{:S(2)}, u32[]{:S(2)}) collective-permute-start(bf16[2,8,1,8,128]{4,3,2,1,0:T(8,128)(2,1)S(1)} %get-tuple-element.120), channel_id=1, source_target_pairs={{1,0},{2,1},{3,2},{5,4},{6,5},{7,6},{9,8},{10,9},{11,10},{13,12},{... | collective-permute-start | bytes 98312 | tf_op jit(solution)/shard_map/ppermute | solution.py:17
  134.7 35.5 %collective-permute-start.5 = (bf16[2,8,1,8,128]{4,3,2,1,0:T(8,128)(2,1)S(1)}, bf16[2,8,1,8,128]{4,3,2,1,0:T(8,128)(2,1)S(1)}, u32[]{:S(2)}, u32[]{:S(2)}) collective-permute-start(bf16[2,8,1,8,128]{4,3,2,1,0:T(8,128)(2,1)S(1)} %get-tuple-element.119), channel_id=1, source_target_pairs={{0,1},{1,2},{2,3},{4,5},{5,6},{6,7},{8,9},{9,10},{10,11},{12,13},{... | collective-permute-start | bytes 98312 | tf_op jit(solution)/shard_map/ppermute | solution.py:17
  139.3 32.6 %collective-permute-start.2 = (bf16[2,1,8,8,128]{4,3,2,1,0:T(8,128)(2,1)S(1)}, bf16[2,1,8,8,128]{4,3,2,1,0:T(8,128)(2,1)S(1)}, u32[]{:S(2)}, u32[]{:S(2)}) collective-permute-start(bf16[2,1,8,8,128]{4,3,2,1,0:T(8,128)(2,1)S(1)} %get-tuple-element.118), channel_id=1, source_target_pairs={{0,4},{4,8},{8,12},{12,16},{16,20},{20,24},{24,28},{28,32},{32,36}... | collective-permute-start | bytes 98312 | tf_op jit(solution)/shard_map/ppermute | solution.py:17
  141.2 32.4 %collective-permute-start.9 = (bf16[2,1,8,8,128]{4,3,2,1,0:T(8,128)(2,1)S(1)}, bf16[2,1,8,8,128]{4,3,2,1,0:T(8,128)(2,1)S(1)}, u32[]{:S(2)}, u32[]{:S(2)}) collective-permute-start(bf16[2,1,8,8,128]{4,3,2,1,0:T(8,128)(2,1)S(1)} %get-tuple-element.117), channel_id=1, source_target_pairs={{4,0},{8,4},{12,8},{16,12},{20,16},{24,20},{28,24},{32,28},{36,32}... | collective-permute-start | bytes 98312 | tf_op jit(solution)/shard_map/ppermute | solution.py:17
  205.0 72.1 %collective-permute-start.17 = (bf16[2,4,1,4,256]{4,3,2,1,0:T(4,128)(2,1)S(1)}, bf16[2,4,1,4,256]{4,3,2,1,0:T(4,128)(2,1)S(1)}, u32[]{:S(2)}, u32[]{:S(2)}) collective-permute-start(bf16[2,4,1,4,256]{4,3,2,1,0:T(4,128)(2,1)S(1)} %get-tuple-element.165), channel_id=1, source_target_pairs={{0,1},{1,2},{2,3},{4,5},{5,6},{6,7},{8,9},{9,10},{10,11},{12,13},{... | collective-permute-start | bytes 49160 | tf_op jit(solution)/shard_map/ppermute | solution.py:17
  235.4 23.1 %collective-permute-start.13 = (bf16[2,1,1,4,256]{4,3,2,1,0:T(4,128)(2,1)S(1)}, bf16[2,1,1,4,256]{4,3,2,1,0:T(4,128)(2,1)S(1)}, u32[]{:S(2)}, u32[]{:S(2)}) collective-permute-start(bf16[2,1,1,4,256]{4,3,2,1,0:T(4,128)(2,1)S(1)} %collective-permute-done.12), channel_id=1, source_target_pairs={{0,1},{1,2},{2,3},{4,5},{5,6},{6,7},{8,9},{9,10},{10,11},{12,13},{... | collective-permute-start | bytes 12296 | tf_op jit(solution)/shard_map/ppermute | solution.py:17
  240.9 38.3 %collective-permute-start.21 = (bf16[2,1,4,4,256]{4,3,2,1,0:T(4,128)(2,1)S(1)}, bf16[2,1,4,4,256]{4,3,2,1,0:T(4,128)(2,1)S(1)}, u32[]{:S(2)}, u32[]{:S(2)}) collective-permute-start(bf16[2,1,4,4,256]{4,3,2,1,0:T(4,128)(2,1)S(1)} %get-tuple-element.161), channel_id=1, source_target_pairs={{4,0},{8,4},{12,8},{16,12},{20,16},{24,20},{28,24},{32,28},{36,32}... | collective-permute-start | bytes 49160 | tf_op jit(solution)/shard_map/ppermute | solution.py:17
  251.6 29.8 %collective-permute-start.18 = (bf16[2,4,1,4,256]{4,3,2,1,0:T(4,128)(2,1)S(1)}, bf16[2,4,1,4,256]{4,3,2,1,0:T(4,128)(2,1)S(1)}, u32[]{:S(2)}, u32[]{:S(2)}) collective-permute-start(bf16[2,4,1,4,256]{4,3,2,1,0:T(4,128)(2,1)S(1)} %get-tuple-element.166), channel_id=1, source_target_pairs={{1,0},{2,1},{3,2},{5,4},{6,5},{7,6},{9,8},{10,9},{11,10},{13,12},{... | collective-permute-start | bytes 49160 | tf_op jit(solution)/shard_map/ppermute | solution.py:17
  255.0 28.2 %collective-permute-start.14 = (bf16[2,1,4,4,256]{4,3,2,1,0:T(4,128)(2,1)S(1)}, bf16[2,1,4,4,256]{4,3,2,1,0:T(4,128)(2,1)S(1)}, u32[]{:S(2)}, u32[]{:S(2)}) collective-permute-start(bf16[2,1,4,4,256]{4,3,2,1,0:T(4,128)(2,1)S(1)} %get-tuple-element.162), channel_id=1, source_target_pairs={{0,4},{4,8},{8,12},{12,16},{16,20},{20,24},{24,28},{28,32},{32,36}... | collective-permute-start | bytes 49160 | tf_op jit(solution)/shard_map/ppermute | solution.py:17
  392.7 716.3 %all-reduce.7.cloned.1.call-start = ((), (), s32[]{:S(2)}) async-start(), calls=%async_computation.2 | async-start | bytes 154624 | tf_op jit(solution)/shard_map/psum | solution.py:192
  392.7 577.8 %collective-permute-start.43 = (bf16[2,1,1,8,128]{4,3,2,1,0:T(8,128)(2,1)S(1)}, bf16[2,1,1,8,128]{4,3,2,1,0:T(8,128)(2,1)S(1)}, u32[]{:S(2)}, u32[]{:S(2)}) collective-permute-start(bf16[2,1,1,8,128]{4,3,2,1,0:T(8,128)(2,1)S(1)} %copy-done.110), channel_id=1, source_target_pairs={{4,0},{8,4},{12,8},{16,12},{20,16},{24,20},{28,24},{32,28},{36,32}... | collective-permute-start | bytes 12296 | tf_op jit(solution)/shard_map/ppermute | solution.py:17
  403.3 609.4 %collective-permute-start.45 = (bf16[2,1,8,8,128]{4,3,2,1,0:T(8,128)(2,1)S(1)}, bf16[2,1,8,8,128]{4,3,2,1,0:T(8,128)(2,1)S(1)}, u32[]{:S(2)}, u32[]{:S(2)}) collective-permute-start(bf16[2,1,8,8,128]{4,3,2,1,0:T(8,128)(2,1)S(1)} %copy-done.33), channel_id=1, source_target_pairs={{4,0},{8,4},{12,8},{16,12},{20,16},{24,20},{28,24},{32,28},{36,32}... | collective-permute-start | bytes 98312 | tf_op jit(solution)/shard_map/ppermute | solution.py:17
  405.2 566.6 %collective-permute-start.46 = (bf16[2,1,1,8,128]{4,3,2,1,0:T(8,128)(2,1)S(1)}, bf16[2,1,1,8,128]{4,3,2,1,0:T(8,128)(2,1)S(1)}, u32[]{:S(2)}, u32[]{:S(2)}) collective-permute-start(bf16[2,1,1,8,128]{4,3,2,1,0:T(8,128)(2,1)S(1)} %copy-done.109), channel_id=1, source_target_pairs={{4,0},{8,4},{12,8},{16,12},{20,16},{24,20},{28,24},{32,28},{36,32}... | collective-permute-start | bytes 12296 | tf_op jit(solution)/shard_map/ppermute | solution.py:17
  407.2 565.9 %collective-permute-start.36 = (bf16[2,1,1,8,128]{4,3,2,1,0:T(8,128)(2,1)S(1)}, bf16[2,1,1,8,128]{4,3,2,1,0:T(8,128)(2,1)S(1)}, u32[]{:S(2)}, u32[]{:S(2)}) collective-permute-start(bf16[2,1,1,8,128]{4,3,2,1,0:T(8,128)(2,1)S(1)} %copy-done.108), channel_id=1, source_target_pairs={{0,4},{4,8},{8,12},{12,16},{16,20},{20,24},{24,28},{28,32},{32,36}... | collective-permute-start | bytes 12296 | tf_op jit(solution)/shard_map/ppermute | solution.py:17
  409.6 579.2 %collective-permute-start.39 = (bf16[2,1,1,8,128]{4,3,2,1,0:T(8,128)(2,1)S(1)}, bf16[2,1,1,8,128]{4,3,2,1,0:T(8,128)(2,1)S(1)}, u32[]{:S(2)}, u32[]{:S(2)}) collective-permute-start(bf16[2,1,1,8,128]{4,3,2,1,0:T(8,128)(2,1)S(1)} %copy-done.107), channel_id=1, source_target_pairs={{0,4},{4,8},{8,12},{12,16},{16,20},{20,24},{24,28},{28,32},{32,36}... | collective-permute-start | bytes 12296 | tf_op jit(solution)/shard_map/ppermute | solution.py:17
  971.8 27.0 %collective-permute-start.47 = (bf16[2,1,1,8,128]{4,3,2,1,0:T(8,128)(2,1)S(1)}, bf16[2,1,1,8,128]{4,3,2,1,0:T(8,128)(2,1)S(1)}, u32[]{:S(2)}, u32[]{:S(2)}) collective-permute-start(bf16[2,1,1,8,128]{4,3,2,1,0:T(8,128)(2,1)S(1)} %collective-permute-done.46), channel_id=1, source_target_pairs={{1,0},{2,1},{3,2},{5,4},{6,5},{7,6},{9,8},{10,9},{11,10},{13,12},{... | collective-permute-start | bytes 12296 | tf_op jit(solution)/shard_map/ppermute | solution.py:17
  973.1 29.0 %collective-permute-start.37 = (bf16[2,1,1,8,128]{4,3,2,1,0:T(8,128)(2,1)S(1)}, bf16[2,1,1,8,128]{4,3,2,1,0:T(8,128)(2,1)S(1)}, u32[]{:S(2)}, u32[]{:S(2)}) collective-permute-start(bf16[2,1,1,8,128]{4,3,2,1,0:T(8,128)(2,1)S(1)} %collective-permute-done.36), channel_id=1, source_target_pairs={{0,1},{1,2},{2,3},{4,5},{5,6},{6,7},{8,9},{9,10},{10,11},{12,13},{... | collective-permute-start | bytes 12296 | tf_op jit(solution)/shard_map/ppermute | solution.py:17
  (130 other events, 10625.3 us)
Sparse Core Ops, SparseCore 0:
  392.8 414.3 reduce-scatter.3
  1051.5 57.4 all-reduce.6
where the time goes:
time: 1120 us
  blocking collectives  547 us (49%)
  local copies, waits for them, and re-layouts  194 us (17%)
  starting transfers between devices  183 us (16%)
  other arithmetic  95.3 us (9%)
  waiting for transfers between devices  54.4 us (5%)
  matrix products  26.9 us (2%)
  between operations  19 us (2%)
    unnamed x1, blocking collectives  547 us
    ppermute x48, starting transfers between devices, shifted(): return lax.ppermute(block, axis, route)  183 us
    unnamed x326, local copies, waits for them, and re-layouts  76.4 us
    gather x104, local copies, waits for them, and re-layouts, surround(): picked = jnp.take(source, jnp.maximum(slot_ids, 0), axis=0)  65.7 us
    select_n x66, other arithmetic, surround(): jnp.where((slot_ids >= 0)[:, None, None, None, None], picked, jnp.zeros((...  57.1 us
    psum x1, waiting for transfers between devices, body(): lax.psum(columns[0].astype(jnp.bfloat16), 'gy').astype(jnp.float32)  51.8 us
  transfers between devices with their start and end apart: 50, of which 3 were waited for; matrix products, arithmetic and copies ran while one was open for 15% of the time, Pallas kernels for 0%

commit v1 on v0

--- a/solution.py
+++ b/solution.py
@@ -189,7 +189,7 @@
         lax.psum_scatter(second_term, "gx", scatter_dimension=1, tiled=True),
     )
     summed = (
-        lax.psum(columns[0].astype(jnp.bfloat16), "gy").astype(jnp.float32),
+        jnp.sum(lax.all_gather(columns[0].astype(jnp.bfloat16), "gy"), axis=0).astype(jnp.float32),
         lax.psum(columns[1].astype(jnp.bfloat16), "gy").astype(jnp.float32),
         lax.psum(columns[2].astype(jnp.bfloat16), "gy").astype(jnp.float32),
     )

time: 1120 us -> 1090 us (0.973)
  blocking collectives: 547 us -> 599 us
  waiting for transfers between devices: 54.4 us -> 2.54 us
  local copies, waits for them, and re-layouts: 194 us -> 175 us
  starting transfers between devices: 183 us -> 169 us
    psum x1 -> x0, waiting for transfers between devices: 51.8 us -> none  [body(): lax.psum(columns[0].astype(jnp.bfloat16), 'gy').astype(jnp.float32)]
    all_gather x0 -> x1, blocking collectives: none -> 23.3 us  [body(): lax.all_gather(columns[0].astype(jnp.bfloat16), 'gy')]
    psum x0 -> x1, blocking collectives: none -> 20.9 us  [body(): lax.psum(columns[1].astype(jnp.bfloat16), 'gy').astype(jnp.float32)]
    unnamed x326, local copies, waits for them, and re-layouts: 76.4 us -> 59 us
    ppermute x48, starting transfers between devices: 183 us -> 169 us  [shifted(): return lax.ppermute(block, axis, route)]
  transfers between devices with their start and end apart: 50 -> 49, of which waited for: 3 -> 2; matrix products, arithmetic and copies ran while one was open for 15% -> 14% of each run, Pallas kernels for 0% -> 0%
where the time goes in v1:
time: 1090 us; the launch traced here: 1080 us
  blocking collectives  599 us (55%)
  local copies, waits for them, and re-layouts  175 us (16%)
  starting transfers between devices  169 us (16%)
  other arithmetic  93.1 us (9%)
  matrix products  23.7 us (2%)
  between operations  19.5 us (2%)
    unnamed x1, blocking collectives  554 us
    ppermute x48, starting transfers between devices, shifted(): return lax.ppermute(block, axis, route)  169 us
    gather x104, local copies, waits for them, and re-layouts, surround(): picked = jnp.take(source, jnp.maximum(slot_ids, 0), axis=0)  65.7 us
    unnamed x326, local copies, waits for them, and re-layouts  59 us
    select_n x66, other arithmetic, surround(): jnp.where((slot_ids >= 0)[:, None, None, None, None], picked, jnp.zeros((...  57.4 us
    all_gather x1, blocking collectives, body(): lax.all_gather(columns[0].astype(jnp.bfloat16), 'gy')  23.3 us
  transfers between devices with their start and end apart: 49, of which 2 were waited for; matrix products, arithmetic and copies ran while one was open for 14% of the time, Pallas kernels for 0%

profile of v1, /device:TPU:2, one launch (start us, length us, event | category | flops | bytes accessed | tf_op | source)
XLA Modules:
  0.0 1081.1 jit_solution(12026432976370951578)
XLA Ops:
  10.9 9.2 collective-permute-start
  20.1 3.7 collective-permute-start.7
  27.4 7.5 collective-permute-start.31
  63.6 4.3 collective-permute-start.1
  67.9 2.9 collective-permute-start.8
  73.4 5.7 copy.23
  79.2 4.2 rev.6
  89.3 4.5 collective-permute-start.29
  101.1 3.6 collective-permute-start.32
  115.1 9.1 collective-permute-start.33
  126.8 5.5 collective-permute-start.25
  134.9 4.6 collective-permute-start.5
  141.4 10.6 collective-permute-start.9
  190.0 3.0 multiply_convert_fusion.1
  195.3 10.3 copy.26
  205.6 3.9 collective-permute-start.17
  209.6 10.3 collective-permute-start.19
  227.1 3.9 collective-permute-start.20
  236.0 3.9 collective-permute-start.13
  241.6 8.6 collective-permute-start.21
  327.2 5.0 fusion.3
  382.8 3.8 copy.29
  386.6 5.3 fusion.61
  393.3 554.4 %all-reduce.5 = (bf16[27,128,128]{2,1,0:T(8,128)(2,1)}, bf16[27,256,256]{2,1,0:T(8,128)(2,1)}) all-reduce(f32[27,128,128]{2,1,0:T(8,128)S(1)} %fusion.3, f32[27,256,256]{2,1,0:T(8,128)} %fusion.61), channel_id=3, replica_groups=mesh['gx'=64,'gy'=4] {'gx'}, use_global_device_ids=true, to_apply=%region_0.9.clone | all-reduce | flops 2211840 | bytes 13271040
  948.6 23.3 %all-gather = bf16[108,2,128]{2,1,0:T(2,128)(2,1)S(1)} all-gather(bf16[27,2,128]{2,1,0:T(2,128)(2,1)S(1)} %dynamic-slice_convert_fusion.1), channel_id=2, replica_groups=mesh['gx'=64,'gy'=4] {'gy'}, dimensions={0}, use_global_device_ids=true | all-gather | bytes 69120 | tf_op jit(solution)/shard_map/all_gather | solution.py:192
  972.6 4.9 collective-permute-start.43
  983.8 7.5 collective-permute-start.39
  991.4 3.2 convolution_convert_fusion.1
  996.1 3.3 collective-permute-start.44
  1000.7 4.5 collective-permute-start.37
  1008.2 4.5 collective-permute-start.41
  1051.9 20.9 %all-reduce.3 = (bf16[8,2,256]{2,0,1:T(8,128)(2,1)S(1)}, bf16[27,4,256]{2,1,0:T(4,128)(2,1)S(1)}) all-reduce(bf16[8,2,256]{2,0,1:T(8,128)(2,1)S(1)} %convert_element_type.46, bf16[27,4,256]{2,1,0:T(4,128)(2,1)S(1)} %dynamic-slice_convert_fusion), channel_id=1, replica_groups=mesh['gx'=64,'gy'=4] {'gy'}, use_global_device_ids=true, to_apply=%region_3.12 | all-reduce | flops 31744 | bytes 126976 | tf_op jit(solution)/shard_map/psum | solution.py:193
  (751 shorter events, 301.5 us)
Async XLA Ops:
  7.2 1043.9 %reduce-scatter.4.cloned.1.call-start = ((), (), s32[]{:S(2)}) async-start(), calls=%async_computation.1 | async-start | bytes 1064960 | tf_op jit(solution)/shard_map/reduce_scatter | solution.py:188
  9.0 50.8 %collective-permute-start.3 = (bf16[2,1,1,8,128]{4,3,2,1,0:T(8,128)(2,1)S(1)}, bf16[2,1,1,8,128]{4,3,2,1,0:T(8,128)(2,1)S(1)}, u32[]{:S(2)}, u32[]{:S(2)}) collective-permute-start(bf16[2,1,1,8,128]{4,3,2,1,0:T(8,128)(2,1)S(1)} %get-tuple-element.114), channel_id=1, source_target_pairs={{0,4},{4,8},{8,12},{12,16},{16,20},{20,24},{24,28},{28,32},{32,36}... | collective-permute-start | bytes 12296 | tf_op jit(solution)/shard_map/ppermute | solution.py:17
  10.9 50.2 %collective-permute-start = (bf16[2,1,1,8,128]{4,3,2,1,0:T(8,128)(2,1)S(1)}, bf16[2,1,1,8,128]{4,3,2,1,0:T(8,128)(2,1)S(1)}, u32[]{:S(2)}, u32[]{:S(2)}) collective-permute-start(bf16[2,1,1,8,128]{4,3,2,1,0:T(8,128)(2,1)S(1)} %get-tuple-element.115), channel_id=1, source_target_pairs={{0,4},{4,8},{8,12},{12,16},{16,20},{20,24},{24,28},{28,32},{32,36}... | collective-permute-start | bytes 12296 | tf_op jit(solution)/shard_map/ppermute | solution.py:17
  20.1 43.5 %collective-permute-start.7 = (bf16[2,1,1,8,128]{4,3,2,1,0:T(8,128)(2,1)S(1)}, bf16[2,1,1,8,128]{4,3,2,1,0:T(8,128)(2,1)S(1)}, u32[]{:S(2)}, u32[]{:S(2)}) collective-permute-start(bf16[2,1,1,8,128]{4,3,2,1,0:T(8,128)(2,1)S(1)} %get-tuple-element.112), channel_id=1, source_target_pairs={{4,0},{8,4},{12,8},{16,12},{20,16},{24,20},{28,24},{32,28},{36,32}... | collective-permute-start | bytes 12296 | tf_op jit(solution)/shard_map/ppermute | solution.py:17
  23.8 44.1 %collective-permute-start.10 = (bf16[2,1,1,8,128]{4,3,2,1,0:T(8,128)(2,1)S(1)}, bf16[2,1,1,8,128]{4,3,2,1,0:T(8,128)(2,1)S(1)}, u32[]{:S(2)}, u32[]{:S(2)}) collective-permute-start(bf16[2,1,1,8,128]{4,3,2,1,0:T(8,128)(2,1)S(1)} %get-tuple-element.113), channel_id=1, source_target_pairs={{4,0},{8,4},{12,8},{16,12},{20,16},{24,20},{28,24},{32,28},{36,32}... | collective-permute-start | bytes 12296 | tf_op jit(solution)/shard_map/ppermute | solution.py:17
  27.4 71.2 %collective-permute-start.31 = (bf16[2,1,1,4,256]{4,3,2,1,0:T(4,128)(2,1)S(1)}, bf16[2,1,1,4,256]{4,3,2,1,0:T(4,128)(2,1)S(1)}, u32[]{:S(2)}, u32[]{:S(2)}) collective-permute-start(bf16[2,1,1,4,256]{4,3,2,1,0:T(4,128)(2,1)S(1)} %get-tuple-element.148), channel_id=1, source_target_pairs={{4,0},{8,4},{12,8},{16,12},{20,16},{24,20},{28,24},{32,28},{36,32}... | collective-permute-start | bytes 12296 | tf_op jit(solution)/shard_map/ppermute | solution.py:17
  61.2 39.9 %collective-permute-start.34 = (bf16[2,1,1,4,256]{4,3,2,1,0:T(4,128)(2,1)S(1)}, bf16[2,1,1,4,256]{4,3,2,1,0:T(4,128)(2,1)S(1)}, u32[]{:S(2)}, u32[]{:S(2)}) collective-permute-start(bf16[2,1,1,4,256]{4,3,2,1,0:T(4,128)(2,1)S(1)} %get-tuple-element.149), channel_id=1, source_target_pairs={{4,0},{8,4},{12,8},{16,12},{20,16},{24,20},{28,24},{32,28},{36,32}... | collective-permute-start | bytes 12296 | tf_op jit(solution)/shard_map/ppermute | solution.py:17
  63.6 25.7 %collective-permute-start.1 = (bf16[2,1,1,8,128]{4,3,2,1,0:T(8,128)(2,1)S(1)}, bf16[2,1,1,8,128]{4,3,2,1,0:T(8,128)(2,1)S(1)}, u32[]{:S(2)}, u32[]{:S(2)}) collective-permute-start(bf16[2,1,1,8,128]{4,3,2,1,0:T(8,128)(2,1)S(1)} %collective-permute-done), channel_id=1, source_target_pairs={{0,1},{1,2},{2,3},{4,5},{5,6},{6,7},{8,9},{9,10},{10,11},{12,13},{... | collective-permute-start | bytes 12296 | tf_op jit(solution)/shard_map/ppermute | solution.py:17
  67.9 27.7 %collective-permute-start.8 = (bf16[2,1,1,8,128]{4,3,2,1,0:T(8,128)(2,1)S(1)}, bf16[2,1,1,8,128]{4,3,2,1,0:T(8,128)(2,1)S(1)}, u32[]{:S(2)}, u32[]{:S(2)}) collective-permute-start(bf16[2,1,1,8,128]{4,3,2,1,0:T(8,128)(2,1)S(1)} %collective-permute-done.7), channel_id=1, source_target_pairs={{0,1},{1,2},{2,3},{4,5},{5,6},{6,7},{8,9},{9,10},{10,11},{12,13},{... | collective-permute-start | bytes 12296 | tf_op jit(solution)/shard_map/ppermute | solution.py:17
  70.8 33.9 %collective-permute-start.11 = (bf16[2,1,1,8,128]{4,3,2,1,0:T(8,128)(2,1)S(1)}, bf16[2,1,1,8,128]{4,3,2,1,0:T(8,128)(2,1)S(1)}, u32[]{:S(2)}, u32[]{:S(2)}) collective-permute-start(bf16[2,1,1,8,128]{4,3,2,1,0:T(8,128)(2,1)S(1)} %collective-permute-done.10), channel_id=1, source_target_pairs={{1,0},{2,1},{3,2},{5,4},{6,5},{7,6},{9,8},{10,9},{11,10},{13,12},{... | collective-permute-start | bytes 12296 | tf_op jit(solution)/shard_map/ppermute | solution.py:17
  89.3 50.1 %collective-permute-start.29 = (bf16[2,4,1,4,256]{4,3,2,1,0:T(4,128)(2,1)S(1)}, bf16[2,4,1,4,256]{4,3,2,1,0:T(4,128)(2,1)S(1)}, u32[]{:S(2)}, u32[]{:S(2)}) collective-permute-start(bf16[2,4,1,4,256]{4,3,2,1,0:T(4,128)(2,1)S(1)} %get-tuple-element.154), channel_id=1, source_target_pairs={{0,1},{1,2},{2,3},{4,5},{5,6},{6,7},{8,9},{9,10},{10,11},{12,13},{... | collective-permute-start | bytes 49160 | tf_op jit(solution)/shard_map/ppermute | solution.py:17
  98.6 25.5 %collective-permute-start.24 = (bf16[2,1,1,4,256]{4,3,2,1,0:T(4,128)(2,1)S(1)}, bf16[2,1,1,4,256]{4,3,2,1,0:T(4,128)(2,1)S(1)}, u32[]{:S(2)}, u32[]{:S(2)}) collective-permute-start(bf16[2,1,1,4,256]{4,3,2,1,0:T(4,128)(2,1)S(1)} %get-tuple-element.151), channel_id=1, source_target_pairs={{0,4},{4,8},{8,12},{12,16},{16,20},{20,24},{24,28},{28,32},{32,36}... | collective-permute-start | bytes 12296 | tf_op jit(solution)/shard_map/ppermute | solution.py:17
  101.1 24.4 %collective-permute-start.32 = (bf16[2,1,1,4,256]{4,3,2,1,0:T(4,128)(2,1)S(1)}, bf16[2,1,1,4,256]{4,3,2,1,0:T(4,128)(2,1)S(1)}, u32[]{:S(2)}, u32[]{:S(2)}) collective-permute-start(bf16[2,1,1,4,256]{4,3,2,1,0:T(4,128)(2,1)S(1)} %collective-permute-done.31), channel_id=1, source_target_pairs={{0,1},{1,2},{2,3},{4,5},{5,6},{6,7},{8,9},{9,10},{10,11},{12,13},{... | collective-permute-start | bytes 12296 | tf_op jit(solution)/shard_map/ppermute | solution.py:17
  104.7 22.1 %collective-permute-start.35 = (bf16[2,1,1,4,256]{4,3,2,1,0:T(4,128)(2,1)S(1)}, bf16[2,1,1,4,256]{4,3,2,1,0:T(4,128)(2,1)S(1)}, u32[]{:S(2)}, u32[]{:S(2)}) collective-permute-start(bf16[2,1,1,4,256]{4,3,2,1,0:T(4,128)(2,1)S(1)} %collective-permute-done.34), channel_id=1, source_target_pairs={{1,0},{2,1},{3,2},{5,4},{6,5},{7,6},{9,8},{10,9},{11,10},{13,12},{... | collective-permute-start | bytes 12296 | tf_op jit(solution)/shard_map/ppermute | solution.py:17
  115.1 26.3 %collective-permute-start.33 = (bf16[2,1,4,4,256]{4,3,2,1,0:T(4,128)(2,1)S(1)}, bf16[2,1,4,4,256]{4,3,2,1,0:T(4,128)(2,1)S(1)}, u32[]{:S(2)}, u32[]{:S(2)}) collective-permute-start(bf16[2,1,4,4,256]{4,3,2,1,0:T(4,128)(2,1)S(1)} %get-tuple-element.152), channel_id=1, source_target_pairs={{4,0},{8,4},{12,8},{16,12},{20,16},{24,20},{28,24},{32,28},{36,32}... | collective-permute-start | bytes 49160 | tf_op jit(solution)/shard_map/ppermute | solution.py:17
  124.2 27.8 %collective-permute-start.30 = (bf16[2,4,1,4,256]{4,3,2,1,0:T(4,128)(2,1)S(1)}, bf16[2,4,1,4,256]{4,3,2,1,0:T(4,128)(2,1)S(1)}, u32[]{:S(2)}, u32[]{:S(2)}) collective-permute-start(bf16[2,4,1,4,256]{4,3,2,1,0:T(4,128)(2,1)S(1)} %get-tuple-element.155), channel_id=1, source_target_pairs={{1,0},{2,1},{3,2},{5,4},{6,5},{7,6},{9,8},{10,9},{11,10},{13,12},{... | collective-permute-start | bytes 49160 | tf_op jit(solution)/shard_map/ppermute | solution.py:17
  133.6 35.4 %collective-permute-start.6 = (bf16[2,8,1,8,128]{4,3,2,1,0:T(8,128)(2,1)S(1)}, bf16[2,8,1,8,128]{4,3,2,1,0:T(8,128)(2,1)S(1)}, u32[]{:S(2)}, u32[]{:S(2)}) collective-permute-start(bf16[2,8,1,8,128]{4,3,2,1,0:T(8,128)(2,1)S(1)} %get-tuple-element.119), channel_id=1, source_target_pairs={{1,0},{2,1},{3,2},{5,4},{6,5},{7,6},{9,8},{10,9},{11,10},{13,12},{... | collective-permute-start | bytes 98312 | tf_op jit(solution)/shard_map/ppermute | solution.py:17
  134.9 35.8 %collective-permute-start.5 = (bf16[2,8,1,8,128]{4,3,2,1,0:T(8,128)(2,1)S(1)}, bf16[2,8,1,8,128]{4,3,2,1,0:T(8,128)(2,1)S(1)}, u32[]{:S(2)}, u32[]{:S(2)}) collective-permute-start(bf16[2,8,1,8,128]{4,3,2,1,0:T(8,128)(2,1)S(1)} %get-tuple-element.118), channel_id=1, source_target_pairs={{0,1},{1,2},{2,3},{4,5},{5,6},{6,7},{8,9},{9,10},{10,11},{12,13},{... | collective-permute-start | bytes 98312 | tf_op jit(solution)/shard_map/ppermute | solution.py:17
  139.5 32.9 %collective-permute-start.2 = (bf16[2,1,8,8,128]{4,3,2,1,0:T(8,128)(2,1)S(1)}, bf16[2,1,8,8,128]{4,3,2,1,0:T(8,128)(2,1)S(1)}, u32[]{:S(2)}, u32[]{:S(2)}) collective-permute-start(bf16[2,1,8,8,128]{4,3,2,1,0:T(8,128)(2,1)S(1)} %get-tuple-element.117), channel_id=1, source_target_pairs={{0,4},{4,8},{8,12},{12,16},{16,20},{20,24},{24,28},{28,32},{32,36}... | collective-permute-start | bytes 98312 | tf_op jit(solution)/shard_map/ppermute | solution.py:17
  141.4 32.7 %collective-permute-start.9 = (bf16[2,1,8,8,128]{4,3,2,1,0:T(8,128)(2,1)S(1)}, bf16[2,1,8,8,128]{4,3,2,1,0:T(8,128)(2,1)S(1)}, u32[]{:S(2)}, u32[]{:S(2)}) collective-permute-start(bf16[2,1,8,8,128]{4,3,2,1,0:T(8,128)(2,1)S(1)} %get-tuple-element.116), channel_id=1, source_target_pairs={{4,0},{8,4},{12,8},{16,12},{20,16},{24,20},{28,24},{32,28},{36,32}... | collective-permute-start | bytes 98312 | tf_op jit(solution)/shard_map/ppermute | solution.py:17
  205.6 72.1 %collective-permute-start.17 = (bf16[2,4,1,4,256]{4,3,2,1,0:T(4,128)(2,1)S(1)}, bf16[2,4,1,4,256]{4,3,2,1,0:T(4,128)(2,1)S(1)}, u32[]{:S(2)}, u32[]{:S(2)}) collective-permute-start(bf16[2,4,1,4,256]{4,3,2,1,0:T(4,128)(2,1)S(1)} %get-tuple-element.164), channel_id=1, source_target_pairs={{0,1},{1,2},{2,3},{4,5},{5,6},{6,7},{8,9},{9,10},{10,11},{12,13},{... | collective-permute-start | bytes 49160 | tf_op jit(solution)/shard_map/ppermute | solution.py:17
  231.0 21.2 %collective-permute-start.23 = (bf16[2,1,1,4,256]{4,3,2,1,0:T(4,128)(2,1)S(1)}, bf16[2,1,1,4,256]{4,3,2,1,0:T(4,128)(2,1)S(1)}, u32[]{:S(2)}, u32[]{:S(2)}) collective-permute-start(bf16[2,1,1,4,256]{4,3,2,1,0:T(4,128)(2,1)S(1)} %collective-permute-done.22), channel_id=1, source_target_pairs={{1,0},{2,1},{3,2},{5,4},{6,5},{7,6},{9,8},{10,9},{11,10},{13,12},{... | collective-permute-start | bytes 12296 | tf_op jit(solution)/shard_map/ppermute | solution.py:17
  233.6 22.0 %collective-permute-start.16 = (bf16[2,1,1,4,256]{4,3,2,1,0:T(4,128)(2,1)S(1)}, bf16[2,1,1,4,256]{4,3,2,1,0:T(4,128)(2,1)S(1)}, u32[]{:S(2)}, u32[]{:S(2)}) collective-permute-start(bf16[2,1,1,4,256]{4,3,2,1,0:T(4,128)(2,1)S(1)} %collective-permute-done.15), channel_id=1, source_target_pairs={{1,0},{2,1},{3,2},{5,4},{6,5},{7,6},{9,8},{10,9},{11,10},{13,12},{... | collective-permute-start | bytes 12296 | tf_op jit(solution)/shard_map/ppermute | solution.py:17
  236.0 23.1 %collective-permute-start.13 = (bf16[2,1,1,4,256]{4,3,2,1,0:T(4,128)(2,1)S(1)}, bf16[2,1,1,4,256]{4,3,2,1,0:T(4,128)(2,1)S(1)}, u32[]{:S(2)}, u32[]{:S(2)}) collective-permute-start(bf16[2,1,1,4,256]{4,3,2,1,0:T(4,128)(2,1)S(1)} %collective-permute-done.12), channel_id=1, source_target_pairs={{0,1},{1,2},{2,3},{4,5},{5,6},{6,7},{8,9},{9,10},{10,11},{12,13},{... | collective-permute-start | bytes 12296 | tf_op jit(solution)/shard_map/ppermute | solution.py:17
  241.6 38.3 %collective-permute-start.21 = (bf16[2,1,4,4,256]{4,3,2,1,0:T(4,128)(2,1)S(1)}, bf16[2,1,4,4,256]{4,3,2,1,0:T(4,128)(2,1)S(1)}, u32[]{:S(2)}, u32[]{:S(2)}) collective-permute-start(bf16[2,1,4,4,256]{4,3,2,1,0:T(4,128)(2,1)S(1)} %get-tuple-element.160), channel_id=1, source_target_pairs={{4,0},{8,4},{12,8},{16,12},{20,16},{24,20},{28,24},{32,28},{36,32}... | collective-permute-start | bytes 49160 | tf_op jit(solution)/shard_map/ppermute | solution.py:17
  252.3 29.7 %collective-permute-start.18 = (bf16[2,4,1,4,256]{4,3,2,1,0:T(4,128)(2,1)S(1)}, bf16[2,4,1,4,256]{4,3,2,1,0:T(4,128)(2,1)S(1)}, u32[]{:S(2)}, u32[]{:S(2)}) collective-permute-start(bf16[2,4,1,4,256]{4,3,2,1,0:T(4,128)(2,1)S(1)} %get-tuple-element.165), channel_id=1, source_target_pairs={{1,0},{2,1},{3,2},{5,4},{6,5},{7,6},{9,8},{10,9},{11,10},{13,12},{... | collective-permute-start | bytes 49160 | tf_op jit(solution)/shard_map/ppermute | solution.py:17
  255.7 28.1 %collective-permute-start.14 = (bf16[2,1,4,4,256]{4,3,2,1,0:T(4,128)(2,1)S(1)}, bf16[2,1,4,4,256]{4,3,2,1,0:T(4,128)(2,1)S(1)}, u32[]{:S(2)}, u32[]{:S(2)}) collective-permute-start(bf16[2,1,4,4,256]{4,3,2,1,0:T(4,128)(2,1)S(1)} %get-tuple-element.161), channel_id=1, source_target_pairs={{0,4},{4,8},{8,12},{12,16},{16,20},{20,24},{24,28},{28,32},{32,36}... | collective-permute-start | bytes 49160 | tf_op jit(solution)/shard_map/ppermute | solution.py:17
  972.6 23.6 %collective-permute-start.43 = (bf16[2,1,1,8,128]{4,3,2,1,0:T(8,128)(2,1)S(1)}, bf16[2,1,1,8,128]{4,3,2,1,0:T(8,128)(2,1)S(1)}, u32[]{:S(2)}, u32[]{:S(2)}) collective-permute-start(bf16[2,1,1,8,128]{4,3,2,1,0:T(8,128)(2,1)S(1)} %copy-done.110), channel_id=1, source_target_pairs={{4,0},{8,4},{12,8},{16,12},{20,16},{24,20},{28,24},{32,28},{36,32}... | collective-permute-start | bytes 12296 | tf_op jit(solution)/shard_map/ppermute | solution.py:17
  977.5 51.3 %collective-permute-start.45 = (bf16[2,1,8,8,128]{4,3,2,1,0:T(8,128)(2,1)S(1)}, bf16[2,1,8,8,128]{4,3,2,1,0:T(8,128)(2,1)S(1)}, u32[]{:S(2)}, u32[]{:S(2)}) collective-permute-start(bf16[2,1,8,8,128]{4,3,2,1,0:T(8,128)(2,1)S(1)} %copy-done.33), channel_id=1, source_target_pairs={{4,0},{8,4},{12,8},{16,12},{20,16},{24,20},{28,24},{32,28},{36,32}... | collective-permute-start | bytes 98312 | tf_op jit(solution)/shard_map/ppermute | solution.py:17
  979.4 20.0 %collective-permute-start.46 = (bf16[2,1,1,8,128]{4,3,2,1,0:T(8,128)(2,1)S(1)}, bf16[2,1,1,8,128]{4,3,2,1,0:T(8,128)(2,1)S(1)}, u32[]{:S(2)}, u32[]{:S(2)}) collective-permute-start(bf16[2,1,1,8,128]{4,3,2,1,0:T(8,128)(2,1)S(1)} %copy-done.109), channel_id=1, source_target_pairs={{4,0},{8,4},{12,8},{16,12},{20,16},{24,20},{28,24},{32,28},{36,32}... | collective-permute-start | bytes 12296 | tf_op jit(solution)/shard_map/ppermute | solution.py:17
  983.8 21.5 %collective-permute-start.39 = (bf16[2,1,1,8,128]{4,3,2,1,0:T(8,128)(2,1)S(1)}, bf16[2,1,1,8,128]{4,3,2,1,0:T(8,128)(2,1)S(1)}, u32[]{:S(2)}, u32[]{:S(2)}) collective-permute-start(bf16[2,1,1,8,128]{4,3,2,1,0:T(8,128)(2,1)S(1)} %copy-done.107), channel_id=1, source_target_pairs={{0,4},{4,8},{8,12},{12,16},{16,20},{20,24},{24,28},{28,32},{32,36}... | collective-permute-start | bytes 12296 | tf_op jit(solution)/shard_map/ppermute | solution.py:17
  1008.2 22.0 %collective-permute-start.41 = (bf16[2,8,1,8,128]{4,3,2,1,0:T(8,128)(2,1)S(1)}, bf16[2,8,1,8,128]{4,3,2,1,0:T(8,128)(2,1)S(1)}, u32[]{:S(2)}, u32[]{:S(2)}) collective-permute-start(bf16[2,8,1,8,128]{4,3,2,1,0:T(8,128)(2,1)S(1)} %copy-done.32), channel_id=1, source_target_pairs={{0,1},{1,2},{2,3},{4,5},{5,6},{6,7},{8,9},{9,10},{10,11},{12,13},{... | collective-permute-start | bytes 98312 | tf_op jit(solution)/shard_map/ppermute | solution.py:17
  (129 other events, 10096.3 us)
Sparse Core Ops, SparseCore 0:
  393.4 404.4 reduce-scatter.3
